TPU v7x, 256 devices: a whole 4x4x8 slice. The times are simulated.
256 devices in a mesh: tm: 32 (over y, x, core), tensor: 8 (over z).
Axes of the slice: x: 4, y: 4, z: 8, core: 2. Of those that a mesh axis runs over, the one named last changes fastest.
Arguments:
- features: bfloat16 [32768, 1536], P(('tm', 'tensor')), may hold values from -4 to 4
- frame_mask: int32 [32768], P('tm'), may hold values 0 or 1
- total_length: int32 [1], replicated, may hold values from 24576 to 32768
- norm_gain: float32 [1536], replicated, may hold values from 0.1 to 1.9
- value_weight: bfloat16 [1536, 1536], P(None, 'tensor'), may hold values from -0.15625 to 0.15625
- gate_weight: bfloat16 [1536, 1536], P(None, 'tensor'), may hold values from -0.15625 to 0.15625
- depth_kernel: float32 [31, 1536], P(None, 'tensor'), may hold values from -1 to 1
- batch_gain: float32 [1536], P('tensor'), may hold values from 0.1 to 1.9
- batch_bias: float32 [1536], P('tensor'), may hold values from -2 to 2
- out_weight: bfloat16 [1536, 1536], P('tensor'), may hold values from -0.15625 to 0.15625
- feed_gain: float32 [1536], replicated, may hold values from 0.1 to 1.9
- up_weight: bfloat16 [1536, 6144], P('tm', 'tensor'), may hold values from -0.15625 to 0.15625
- down_weight: bfloat16 [6144, 1536], P('tensor', 'tm'), may hold values from -0.078125 to 0.078125
Outputs:
- encoded: bfloat16 [32768, 1536], P(('tm', 'tensor'))
All inputs are finite; a program needn't handle non-finite values. No bound on the sum of `frame_mask` on one device may be relied on, other than what follows from the above.
Results may differ from a plain program's by a relative error of at most 0.0074.
Values may be sent and summed in bfloat16 or wider, within the bound.
No kernel may reach another device: no remote copies, remote signals or barrier semaphores. Data moves between devices by JAX's collectives and lax.ppermute only.
A program may use at most 64 MiB of HBM per device.

v0:
```python
import jax
import jax.numpy as jnp
from jax import lax
from jax.sharding import PartitionSpec as P

KERNEL = 31


def extended(array, sides, width):
    for axis, dim in sides:
        devices, length = (lax.axis_size(axis), array.shape[dim])
        up = [(i, (i + 1) % devices) for i in range(devices - 1)]
        down = [(j, i) for i, j in up]
        last = lax.slice_in_dim(array, length - width, length, axis=dim)
        initial = lax.slice_in_dim(array, 0, width, axis=dim)
        before = lax.ppermute(last, axis, up)
        after = lax.ppermute(initial, axis, down)
        array = jnp.concatenate([before, array, after], axis=dim)
    return array


def layer_norm(rows, gain):
    values = rows.astype(jnp.float32)
    centre = jnp.mean(values, axis=-1, keepdims=True)
    spread = jnp.mean(jnp.square(values - centre), axis=-1, keepdims=True)
    return (values - centre) * lax.rsqrt(spread + 1e-05) * gain


def merge_moments(low, high):
    n_a, mean_a, m2_a = (low[0], low[1], low[2])
    n_b, mean_b, m2_b = (high[0], high[1], high[2])
    n = n_a + n_b
    share = jnp.where(n > 0, n_b / jnp.maximum(n, 1.0), 0.0)
    delta = mean_b - mean_a
    mean = mean_a + delta * share
    m2 = m2_a + m2_b + jnp.square(delta) * n_a * share
    return jnp.stack([n, mean, m2])


def moments_over(stats, axis):
    size = lax.axis_size(axis)
    me = lax.axis_index(axis)
    step = 1
    while step < size:
        pairs = [(i, i ^ step) for i in range(size)]
        other = lax.ppermute(stats, axis, pairs)
        mine_low = me & step == 0
        low = jnp.where(mine_low, stats, other)
        high = jnp.where(mine_low, other, stats)
        stats = merge_moments(low, high)
        step *= 2
    return stats


def shards(
    features,
    frame_mask,
    total_length,
    norm_gain,
    value_weight,
    gate_weight,
    depth_kernel,
    batch_gain,
    batch_bias,
    out_weight,
    feed_gain,
    up_weight,
    down_weight,
):
    own_rows = features.shape[0]
    block = own_rows * lax.axis_size("tensor")
    positions = lax.axis_index("tm") * block + jnp.arange(block, dtype=jnp.int32)
    valid = ((frame_mask > 0) & (positions < total_length[0])).astype(jnp.float32)
    normed = layer_norm(features, norm_gain).astype(jnp.bfloat16)
    piece = lax.all_gather(normed, "tensor", axis=0, tiled=True)
    up_whole = lax.all_gather(up_weight, "tm", axis=0, tiled=True)
    down_whole = lax.all_gather(down_weight, "tm", axis=1, tiled=True)
    value = jnp.dot(piece, value_weight, preferred_element_type=jnp.float32)
    gate = jnp.dot(piece, gate_weight, preferred_element_type=jnp.float32)
    glu = (value * jax.nn.sigmoid(gate) * valid[:, None]).astype(jnp.bfloat16)
    padded = extended(glu, (("tm", 0),), KERNEL // 2)
    conv = jnp.zeros(glu.shape, jnp.float32)
    for tap in range(KERNEL):
        conv = conv + padded[tap : tap + block].astype(jnp.float32) * depth_kernel[tap]
    count_local = jnp.sum(valid)
    local_sum = jnp.sum(conv * valid[:, None], axis=0)
    local_mean = jnp.where(count_local > 0, local_sum / jnp.maximum(count_local, 1.0), 0.0)
    local_m2 = jnp.sum(jnp.square(conv - local_mean) * valid[:, None], axis=0)
    stats = jnp.stack([jnp.broadcast_to(count_local, local_sum.shape), local_mean, local_m2])
    stats = moments_over(stats, "tm")
    count, mean, m2 = (stats[0], stats[1], stats[2])
    centred = conv - mean
    var = m2 / count
    scaled = centred * lax.rsqrt(var + 1e-05) * batch_gain + batch_bias
    swished = (scaled * jax.nn.sigmoid(scaled)).astype(jnp.bfloat16)
    conv_part = jnp.dot(swished, out_weight, preferred_element_type=jnp.float32)
    conv_part, up_whole, down_whole = lax.optimization_barrier((conv_part, up_whole, down_whole))
    conv_out = lax.psum_scatter(
        conv_part.astype(jnp.bfloat16), "tensor", scatter_dimension=0, tiled=True
    ).astype(jnp.float32)
    mid = (features.astype(jnp.float32) + conv_out).astype(jnp.bfloat16)
    feed_normed = layer_norm(mid, feed_gain).astype(jnp.bfloat16)
    feed_block = lax.all_gather(feed_normed, "tensor", axis=0, tiled=True)
    pre = jnp.dot(feed_block, up_whole, preferred_element_type=jnp.float32)
    hidden = (pre * jax.nn.sigmoid(pre)).astype(jnp.bfloat16)
    partial_out = jnp.dot(hidden, down_whole, preferred_element_type=jnp.float32)
    feed_out = lax.psum_scatter(
        partial_out.astype(jnp.bfloat16), "tensor", scatter_dimension=0, tiled=True
    ).astype(jnp.float32)
    return (mid.astype(jnp.float32) + 0.5 * feed_out).astype(jnp.bfloat16)


def solution(mesh):
    placed = (
        P(("tm", "tensor"), None),
        P("tm"),
        P(),
        P(),
        P(None, "tensor"),
        P(None, "tensor"),
        P(None, "tensor"),
        P("tensor"),
        P("tensor"),
        P("tensor", None),
        P(),
        P("tm", "tensor"),
        P("tensor", "tm"),
    )
    return jax.shard_map(
        shards, mesh=mesh, in_specs=placed, out_specs=P(("tm", "tensor"), None), check_vma=False
    )
```

profile of v0, /device:TPU:2, one launch (start us, length us, event | category | flops | bytes accessed | tf_op | source)
XLA Modules:
  0.0 321.7 jit_solution(17575117318898476684)
XLA Ops:
  6.5 1.2 convert_reduce_fusion.1
  7.7 1.2 fusion.13
  9.0 2.0 fusion.15
  11.0 0.0 all-gather.5.cloned.1.call-update
  11.1 0.0 all-gather.7.cloned.1.call-start
  11.1 0.7 all-gather.7.cloned.1.call-update
  11.8 0.0 all-gather.9.cloned.1.call-start
  11.8 0.7 all-gather.9.cloned.1.call-update
  12.5 0.0 reduce-scatter.3.cloned.1.call-start
  13.2 1.0 fusion.66
  14.3 1.4 fusion.63
  15.6 43.5 %all-gather.5.cloned.1.call-done = bf16[1024,1536]{1,0:T(8,128)(2,1)} async-done(((bf16[128,1536]{1,0:T(8,128)(2,1)}), bf16[1024,1536]{1,0:T(8,128)(2,1)}) %all-gather.5.cloned.1.call-update) | async-done | bytes 3145744 | tf_op jit(solution)/shard_map/all_gather | solution.py:75
  59.1 3.4 %fusion.4 = f32[1024,192]{0,1:T(8,128)S(1)} fusion(bf16[1024,1536]{1,0:T(8,128)(2,1)} %all-gather.5.cloned.1.call-done, bf16[1536,192]{0,1:T(8,128)(2,1)} %param.18), kind=kOutput, calls=%fused_computation.36 | convolution fusion | flops 604569600 | bytes 4521984 | tf_op jit(solution)/shard_map/dot_general | solution.py:79
  62.6 1.2 fusion.5
  63.8 0.1 fusion.65
  63.9 1.9 collective-permute-start
  65.8 3.6 %collective-permute-start.1 = (bf16[15,192]{0,1:T(8,128)(2,1)S(1)}, bf16[15,192]{0,1:T(8,128)(2,1)S(1)}, u32[]{:S(2)}, u32[]{:S(2)}) collective-permute-start(bf16[15,192]{0,1:T(8,128)(2,1)S(1)} %get-tuple-element.32), channel_id=1, source_target_pairs={{8,0},{16,8},{24,16},{32,24},{40,32},{48,40},{56,48},{64,56},{72,6... | collective-permute-start | bytes 17288 | tf_op jit(solution)/shard_map/ppermute | solution.py:17
  69.4 1.0 fusion.67
  71.7 0.6 pad.12.clone
  72.4 5.6 %multiply_reduce_fusion.1 = (f32[192]{0:T(256)S(1)}, f32[1024,192]{0,1:T(8,128)S(1)}) fusion(f32[1024]{0:T(1024)S(1)} %get-tuple-element.28, f32[192]{0:T(256)S(1)} %bitcast.79, bf16[15,192]{0,1:T(8,128)(2,1)S(1)} %collective-permute-done.1, bf16[1024,192]{0,1:T(8,128)(2,1)S(1)} %fusion.5, f32[192]{0:T(256)S(1)} %bitcast.80, f32[192]{0:T(256)S(1)} %bitcast.51, ...), kind=kLoop, calls=%fused_computation.58 | loop fusion | flops 36175680 | bytes 1219840 | tf_op jit(solution)/shard_map/reduce_sum | solution.py:86
  78.0 0.3 multiply_reduce_fusion
  78.2 0.1 pad_maximum_fusion.2
  78.3 0.4 collective-permute-start.2
  78.7 0.8 collective-permute-done.2
  79.6 0.1 broadcast_select_fusion.1
  79.7 0.6 collective-permute-start.3
  80.3 3.1 collective-permute-done.3
  83.5 4.3 %collective-permute-start.4 = (f32[3,192]{1,0:T(4,128)S(1)}, f32[3,192]{1,0:T(4,128)S(1)}, u32[]{:S(2)}, u32[]{:S(2)}) collective-permute-start(f32[3,192]{1,0:T(4,128)S(1)} %pad_maximum_fusion.4), channel_id=1, source_target_pairs={{0,32},{8,40},{16,48},{24,56},{32,0},{40,8},{48,16},{56,24},{64,96... | collective-permute-start | bytes 6920 | tf_op jit(solution)/shard_map/ppermute | solution.py:46
  87.7 1.6 collective-permute-done.4
  89.4 1.6 collective-permute-start.5
  91.0 2.1 collective-permute-done.5
  93.2 3.2 collective-permute-start.6
  96.4 2.3 collective-permute-done.6
  98.7 2.9 fusion.18
  101.6 7.7 %all-gather.7.cloned.1.call-done = bf16[1536,768]{1,0:T(8,128)(2,1)} async-done(((bf16[48,768]{1,0:T(8,128)(2,1)}), bf16[1536,768]{1,0:T(8,128)(2,1)}) %all-gather.7.cloned.1.call-update) | async-done | bytes 2359312 | tf_op jit(solution)/shard_map/all_gather | solution.py:76
  109.3 51.2 %all-gather.9.cloned.1.call-done = bf16[768,1536]{0,1:T(8,128)(2,1)} async-done(((bf16[768,48]{0,1:T(8,128)(2,1)}), bf16[768,1536]{0,1:T(8,128)(2,1)}) %all-gather.9.cloned.1.call-update) | async-done | bytes 2359312 | tf_op jit(solution)/shard_map/all_gather | solution.py:77
  160.5 0.0 reduce-scatter.3.cloned.1.call-update
  160.5 0.0 all-gather.11.cloned.1.call-start
  160.6 48.8 %reduce-scatter.3.cloned.1.call-done = bf16[128,1536]{1,0:T(8,128)(2,1)} async-done(((bf16[1024,1536]{1,0:T(8,128)(2,1)}), bf16[128,1536]{1,0:T(8,128)(2,1)}) %reduce-scatter.3.cloned.1.call-update) | async-done | bytes 393232 | tf_op jit(solution)/shard_map/reduce_scatter | solution.py:98
  209.3 1.2 convert_reduce_fusion
  210.6 0.3 fusion.10
  210.8 1.0 fusion.12
  211.9 0.0 all-gather.11.cloned.1.call-update
  211.9 0.0 reduce-scatter.5.cloned.1.call-start
  211.9 44.4 %all-gather.11.cloned.1.call-done = bf16[1024,1536]{1,0:T(8,128)(2,1)} async-done(((bf16[128,1536]{1,0:T(8,128)(2,1)}), bf16[1024,1536]{1,0:T(8,128)(2,1)}) %all-gather.11.cloned.1.call-update) | async-done | bytes 3145744 | tf_op jit(solution)/shard_map/all_gather | solution.py:103
  256.4 11.1 %convolution_convert_fusion = bf16[1024,1536]{1,0:T(8,128)(2,1)} fusion(bf16[768,1536]{0,1:T(8,128)(2,1)} %all-gather.9.cloned.1.call-done, bf16[1024,1536]{1,0:T(8,128)(2,1)} %all-gather.11.cloned.1.call-done, bf16[1536,768]{1,0:T(8,128)(2,1)} %all-gather.7.cloned.1.call-done), kind=kOutput, calls=%fused_computation | convolution fusion | flops 4837343232 | bytes 11010048 | tf_op jit(solution)/shard_map/dot_general | solution.py:106
  267.4 45.6 %reduce-scatter.5.cloned.1.call-done = bf16[128,1536]{1,0:T(8,128)(2,1)} async-done(((bf16[1024,1536]{1,0:T(8,128)(2,1)}), bf16[128,1536]{1,0:T(8,128)(2,1)}) %reduce-scatter.5.cloned.1.call-update) | async-done | bytes 393232 | tf_op jit(solution)/shard_map/reduce_scatter | solution.py:107
  313.0 1.9 fusion.17
  (41 shorter events, 0.3 us)
Async XLA Ops:
  6.5 92.2 %copy-start = (bf16[192,1536]{1,0:T(8,128)(2,1)S(1)}, bf16[192,1536]{1,0:T(8,128)(2,1)}, u32[]{:S(2)}) copy-start(bf16[192,1536]{1,0:T(8,128)(2,1)} %param.22) | copy-start | bytes 1769476
  6.5 52.6 %all-gather.5.cloned.1.call-start = ((), (), s32[]{:S(2)}) async-start(), calls=%async_computation.2 | async-start | bytes 3538944 | tf_op jit(solution)/shard_map/all_gather | solution.py:75
  11.1 98.3 %all-gather.7.cloned.1.call-start = ((), (), s32[]{:S(2)}) async-start(), calls=%async_computation.3 | async-start | bytes 2433024 | tf_op jit(solution)/shard_map/all_gather | solution.py:76
  11.8 148.7 %all-gather.9.cloned.1.call-start = ((), (), s32[]{:S(2)}) async-start(), calls=%async_computation.4 | async-start | bytes 2433024 | tf_op jit(solution)/shard_map/all_gather | solution.py:77
  12.5 196.8 %reduce-scatter.3.cloned.1.call-start = ((), (), s32[]{:S(2)}) async-start(), calls=%async_computation.5 | async-start | bytes 3538944 | tf_op jit(solution)/shard_map/reduce_scatter | solution.py:98
  15.6 46.9 %copy-start.4 = (bf16[1536,192]{0,1:T(8,128)(2,1)S(1)}, bf16[1536,192]{0,1:T(8,128)(2,1)}, u32[]{:S(2)}) copy-start(bf16[1536,192]{0,1:T(8,128)(2,1)} %param.17) | copy-start | bytes 1769476
  59.1 3.4 %copy-start.3 = (bf16[1024,1536]{1,0:T(8,128)(2,1)S(1)}, bf16[1024,1536]{1,0:T(8,128)(2,1)}, u32[]{:S(2)}) copy-start(bf16[1024,1536]{1,0:T(8,128)(2,1)} %all-gather.5.cloned.1.call-done) | copy-start | bytes 9437188
  62.6 36.1 %copy-start.5 = (f32[192]{0:T(256)S(1)}, f32[192]{0:T(256)}, u32[]{:S(2)}) copy-start(f32[192]{0:T(256)} %param.21) | copy-start | bytes 2308
  62.6 36.1 %copy-start.6 = (f32[192]{0:T(256)S(1)}, f32[192]{0:T(256)}, u32[]{:S(2)}) copy-start(f32[192]{0:T(256)} %param.20) | copy-start | bytes 2308
  63.9 8.5 %collective-permute-start = (bf16[15,192]{0,1:T(8,128)(2,1)S(1)}, bf16[15,192]{0,1:T(8,128)(2,1)S(1)}, u32[]{:S(2)}, u32[]{:S(2)}) collective-permute-start(bf16[15,192]{0,1:T(8,128)(2,1)S(1)} %get-tuple-element.31), channel_id=1, source_target_pairs={{0,8},{8,16},{16,24},{24,32},{32,40},{40,48},{48,56},{56,64},{64,7... | collective-permute-start | bytes 17288 | tf_op jit(solution)/shard_map/ppermute | solution.py:16
  65.8 6.6 %collective-permute-start.1 = (bf16[15,192]{0,1:T(8,128)(2,1)S(1)}, bf16[15,192]{0,1:T(8,128)(2,1)S(1)}, u32[]{:S(2)}, u32[]{:S(2)}) collective-permute-start(bf16[15,192]{0,1:T(8,128)(2,1)S(1)} %get-tuple-element.32), channel_id=1, source_target_pairs={{8,0},{16,8},{24,16},{32,24},{40,32},{48,40},{56,48},{64,56},{72,6... | collective-permute-start | bytes 17288 | tf_op jit(solution)/shard_map/ppermute | solution.py:17
  78.3 1.2 collective-permute-start.2
  79.7 3.7 %collective-permute-start.3 = (f32[3,192]{1,0:T(4,128)S(1)}, f32[3,192]{1,0:T(4,128)S(1)}, u32[]{:S(2)}, u32[]{:S(2)}) collective-permute-start(f32[3,192]{1,0:T(4,128)S(1)} %pad_maximum_fusion.3), channel_id=1, source_target_pairs={{0,16},{8,24},{16,0},{24,8},{32,48},{40,56},{48,32},{56,40},{64,80... | collective-permute-start | bytes 6920 | tf_op jit(solution)/shard_map/ppermute | solution.py:46
  83.5 5.9 %collective-permute-start.4 = (f32[3,192]{1,0:T(4,128)S(1)}, f32[3,192]{1,0:T(4,128)S(1)}, u32[]{:S(2)}, u32[]{:S(2)}) collective-permute-start(f32[3,192]{1,0:T(4,128)S(1)} %pad_maximum_fusion.4), channel_id=1, source_target_pairs={{0,32},{8,40},{16,48},{24,56},{32,0},{40,8},{48,16},{56,24},{64,96... | collective-permute-start | bytes 6920 | tf_op jit(solution)/shard_map/ppermute | solution.py:46
  89.4 3.7 %collective-permute-start.5 = (f32[3,192]{1,0:T(4,128)S(1)}, f32[3,192]{1,0:T(4,128)S(1)}, u32[]{:S(2)}, u32[]{:S(2)}) collective-permute-start(f32[3,192]{1,0:T(4,128)S(1)} %pad_maximum_fusion.5), channel_id=1, source_target_pairs={{0,64},{8,72},{16,80},{24,88},{32,96},{40,104},{48,112},{56,120},{... | collective-permute-start | bytes 6920 | tf_op jit(solution)/shard_map/ppermute | solution.py:46
  93.2 5.5 %collective-permute-start.6 = (f32[3,192]{1,0:T(4,128)S(1)}, f32[3,192]{1,0:T(4,128)S(1)}, u32[]{:S(2)}, u32[]{:S(2)}) collective-permute-start(f32[3,192]{1,0:T(4,128)S(1)} %pad_maximum_fusion.6), channel_id=1, source_target_pairs={{0,128},{8,136},{16,144},{24,152},{32,160},{40,168},{48,176},{56,1... | collective-permute-start | bytes 6920 | tf_op jit(solution)/shard_map/ppermute | solution.py:46
  101.6 107.8 %copy-start.1 = (bf16[128,1536]{1,0:T(8,128)(2,1)S(1)}, bf16[128,1536]{1,0:T(8,128)(2,1)}, u32[]{:S(2)}) copy-start(bf16[128,1536]{1,0:T(8,128)(2,1)} %param.13) | copy-start | bytes 1179652
  101.6 109.2 %copy-start.2 = (f32[1536]{0:T(1024)S(1)}, f32[1536]{0:T(1024)}, u32[]{:S(2)}) copy-start(f32[1536]{0:T(1024)} %param.23) | copy-start | bytes 18436
  160.5 95.9 %all-gather.11.cloned.1.call-start = ((), (), s32[]{:S(2)}) async-start(), calls=%async_computation.6 | async-start | bytes 3538944 | tf_op jit(solution)/shard_map/all_gather | solution.py:103
  211.9 101.1 %reduce-scatter.5.cloned.1.call-start = ((), (), s32[]{:S(2)}) async-start(), calls=%async_computation.7 | async-start | bytes 3538944 | tf_op jit(solution)/shard_map/reduce_scatter | solution.py:107
Sparse Core Ops, SparseCore 0:
  11.2 47.9 all-gather.4
  61.7 47.5 all-gather.6
  111.8 48.5 all-gather.8
  162.9 46.4 reduce-scatter.2
  212.0 44.3 all-gather.10
  267.6 45.4 reduce-scatter.4
where the time goes:
time: 322 us
  waiting for transfers between devices  253 us (79%)
  matrix products  18.5 us (6%)
  other arithmetic  16.4 us (5%)
  starting transfers between devices  15.9 us (5%)
  between operations  15.7 us (5%)
    all_gather x1, waiting for transfers between devices, shards(): down_whole = lax.all_gather(down_weight, 'tm', axis=1, tiled=True)  51.2 us
    reduce_scatter x1, waiting for transfers between devices, shards(): lax.psum_scatter(conv_part.astype(jnp.bfloat16), 'tensor', scatter_dimens...  48.8 us
    reduce_scatter x1, waiting for transfers between devices, shards(): lax.psum_scatter(partial_out.astype(jnp.bfloat16), 'tensor', scatter_dime...  45.6 us
    all_gather x1, waiting for transfers between devices, shards(): feed_block = lax.all_gather(feed_normed, 'tensor', axis=0, tiled=True)  44.4 us
    all_gather x1, waiting for transfers between devices, shards(): piece = lax.all_gather(normed, 'tensor', axis=0, tiled=True)  43.5 us
    dot_general x1, matrix products, shards(): jnp.dot(hidden, down_whole, preferred_element_type=jnp.float32)  11.1 us
    ppermute x5, starting transfers between devices, moments_over(): other = lax.ppermute(stats, axis, pairs)  10.1 us
    ppermute x5, waiting for transfers between devices, moments_over(): other = lax.ppermute(stats, axis, pairs)  9.85 us
  transfers between devices with their start and end apart: 13, of which 11 were waited for; matrix products, arithmetic and copies ran while one was open for 6% of the time, Pallas kernels for 0%

commit v1 on v0

--- a/solution.py
+++ b/solution.py
@@ -2,6 +2,7 @@
 import jax.numpy as jnp
 from jax import lax
 from jax.sharding import PartitionSpec as P
+from jax.lax import all_to_all, axis_size
 
 KERNEL = 31
 
@@ -72,7 +73,12 @@
     positions = lax.axis_index("tm") * block + jnp.arange(block, dtype=jnp.int32)
     valid = ((frame_mask > 0) & (positions < total_length[0])).astype(jnp.float32)
     normed = layer_norm(features, norm_gain).astype(jnp.bfloat16)
-    piece = lax.all_gather(normed, "tensor", axis=0, tiled=True)
+    axis_n = axis_size("tensor")
+    lanes = []
+    for s in range(normed.ndim):
+        lanes.append(axis_n if s == 0 else 1)
+    field_out = jnp.tile(normed, lanes)
+    piece = all_to_all(field_out, "tensor", split_axis=0, concat_axis=0, tiled=True)
     up_whole = lax.all_gather(up_weight, "tm", axis=0, tiled=True)
     down_whole = lax.all_gather(down_weight, "tm", axis=1, tiled=True)
     value = jnp.dot(piece, value_weight, preferred_element_type=jnp.float32)

time: 322 us -> 296 us (0.919)
  waiting for transfers between devices: 253 us -> 216 us
  starting transfers between devices: 15.9 us -> 25.4 us
    all_to_all x0 -> x1, waiting for transfers between devices: none -> 71 us  [shards(): all_to_all(field_out, 'tensor', split_axis=0, concat_axis=0, tiled=True)]
    all_gather x1, waiting for transfers between devices: 51.2 us -> 0.01 us  [shards(): down_whole = lax.all_gather(down_weight, 'tm', axis=1, tiled=True)]
    all_gather x1 -> x0, waiting for transfers between devices: 43.5 us -> none  [shards(): piece = lax.all_gather(normed, 'tensor', axis=0, tiled=True)]
    all_to_all x0 -> x1, starting transfers between devices: none -> 8.6 us  [shards(): all_to_all(field_out, 'tensor', split_axis=0, concat_axis=0, tiled=True)]
    all_gather x1, waiting for transfers between devices: 7.71 us -> 0.01 us  [shards(): up_whole = lax.all_gather(up_weight, 'tm', axis=0, tiled=True)]
    reduce_scatter x1, waiting for transfers between devices: 48.8 us -> 44 us  [shards(): lax.psum_scatter(conv_part.astype(jnp.bfloat16), 'tensor', scatter_dimens...]
  transfers between devices with their start and end apart: 13 -> 13, of which waited for: 11 -> 9; matrix products, arithmetic and copies ran while one was open for 6% -> 6% of each run, Pallas kernels for 0% -> 0%
where the time goes in v1:
time: 296 us; the launch traced here: 295 us
  waiting for transfers between devices  216 us (73%)
  starting transfers between devices  25.4 us (9%)
  matrix products  20.2 us (7%)
  between operations  15.4 us (5%)
  other arithmetic  15 us (5%)
    all_to_all x1, waiting for transfers between devices, shards(): all_to_all(field_out, 'tensor', split_axis=0, concat_axis=0, tiled=True)  71 us
    reduce_scatter x1, waiting for transfers between devices, shards(): lax.psum_scatter(partial_out.astype(jnp.bfloat16), 'tensor', scatter_dime...  45.6 us
    all_gather x1, waiting for transfers between devices, shards(): feed_block = lax.all_gather(feed_normed, 'tensor', axis=0, tiled=True)  44.6 us
    reduce_scatter x1, waiting for transfers between devices, shards(): lax.psum_scatter(conv_part.astype(jnp.bfloat16), 'tensor', scatter_dimens...  44 us
    ppermute x5, starting transfers between devices, moments_over(): other = lax.ppermute(stats, axis, pairs)  11.1 us
    dot_general x1, matrix products, shards(): jnp.dot(hidden, down_whole, preferred_element_type=jnp.float32)  11 us
    ppermute x5, waiting for transfers between devices, moments_over(): other = lax.ppermute(stats, axis, pairs)  9.72 us
    all_to_all x1, starting transfers between devices, shards(): all_to_all(field_out, 'tensor', split_axis=0, concat_axis=0, tiled=True)  8.6 us
  transfers between devices with their start and end apart: 13, of which 9 were waited for; matrix products, arithmetic and copies ran while one was open for 6% of the time, Pallas kernels for 0%

profile of v1, /device:TPU:2, one launch (start us, length us, event | category | flops | bytes accessed | tf_op | source)
XLA Modules:
  0.0 295.1 jit_solution(12547482134063443312)
XLA Ops:
  6.5 1.2 convert_reduce_fusion.1
  7.7 1.2 fusion.13
  9.0 1.3 fusion.15
  10.3 1.9 tile.2
  12.2 8.6 %all-to-all-start = ((bf16[8,128,1536]{2,1,0:T(8,128)(2,1)}), bf16[8,128,1536]{2,1,0:T(8,128)(2,1)}, u32[]{:S(2)}, u32[]{:S(2)}) async-start(bf16[8,128,1536]{2,1,0:T(8,128)(2,1)} %tile.2), calls=%async_computation | async-start | bytes 6291456 | tf_op jit(solution)/shard_map/all_to_all | solution.py:81
  20.8 0.0 all-gather.4.cloned.1.call-start
  20.9 0.7 all-gather.4.cloned.1.call-update
  21.6 0.0 all-gather.6.cloned.1.call-start
  21.6 0.7 all-gather.6.cloned.1.call-update
  22.3 0.0 reduce-scatter.3.cloned.1.call-start
  23.0 0.7 fusion.63
  23.7 71.0 %all-to-all-done = bf16[8,128,1536]{2,1,0:T(8,128)(2,1)} async-done(((bf16[8,128,1536]{2,1,0:T(8,128)(2,1)}), bf16[8,128,1536]{2,1,0:T(8,128)(2,1)}, u32[]{:S(2)}, u32[]{:S(2)}) %all-to-all-start) | async-done | bytes 3145760 | tf_op jit(solution)/shard_map/all_to_all | solution.py:81
  94.7 3.2 %fusion.4 = f32[1024,192]{0,1:T(8,128)S(1)} fusion(bf16[1024,1536]{1,0:T(8,128)(2,1)} %bitcast, bf16[1536,192]{0,1:T(8,128)(2,1)S(1)} %copy-done.5), kind=kOutput, calls=%fused_computation.36 | convolution fusion | flops 604569600 | bytes 4521984 | tf_op jit(solution)/shard_map/dot_general | solution.py:85
  97.9 0.0 copy-start.7
  97.9 0.0 copy-start.8
  97.9 3.1 %fusion.5 = bf16[1024,192]{0,1:T(8,128)(2,1)S(1)} fusion(f32[1024,192]{0,1:T(8,128)S(1)} %fusion.4, bf16[1024,1536]{1,0:T(8,128)(2,1)} %bitcast, bf16[1536,192]{0,1:T(8,128)(2,1)S(1)} %copy-done.6, f32[1024]{0:T(1024)S(1)} %get-tuple-element.28), kind=kOutput, calls=%fused_computation.37 | convolution fusion | flops 604569600 | bytes 4919296 | tf_op jit(solution)/shard_map/dot_general | solution.py:84
  101.0 0.1 fusion.65
  101.1 1.9 collective-permute-start
  103.1 3.6 %collective-permute-start.1 = (bf16[15,192]{0,1:T(8,128)(2,1)S(1)}, bf16[15,192]{0,1:T(8,128)(2,1)S(1)}, u32[]{:S(2)}, u32[]{:S(2)}) collective-permute-start(bf16[15,192]{0,1:T(8,128)(2,1)S(1)} %get-tuple-element.32), channel_id=1, source_target_pairs={{8,0},{16,8},{24,16},{32,24},{40,32},{48,40},{56,48},{64,56},{72,6... | collective-permute-start | bytes 17288 | tf_op jit(solution)/shard_map/ppermute | solution.py:18
  108.1 0.7 pad.12.clone
  108.8 5.6 %multiply_reduce_fusion.1 = (f32[192]{0:T(256)S(1)}, f32[1024,192]{0,1:T(8,128)S(1)}) fusion(f32[1024]{0:T(1024)S(1)} %get-tuple-element.28, f32[192]{0:T(256)S(1)} %bitcast.80, bf16[15,192]{0,1:T(8,128)(2,1)S(1)} %collective-permute-done.1, bf16[1024,192]{0,1:T(8,128)(2,1)S(1)} %fusion.5, f32[192]{0:T(256)S(1)} %bitcast.81, f32[192]{0:T(256)S(1)} %bitcast.52, ...), kind=kLoop, calls=%fused_computation.58 | loop fusion | flops 36175680 | bytes 1219840 | tf_op jit(solution)/shard_map/reduce_sum | solution.py:92
  114.4 0.3 multiply_reduce_fusion
  114.7 0.1 pad_maximum_fusion.2
  114.7 1.3 collective-permute-start.2
  116.0 0.8 collective-permute-done.2
  116.9 0.1 broadcast_select_fusion.1
  117.0 0.6 collective-permute-start.3
  117.6 3.1 %collective-permute-done.3 = f32[3,192]{1,0:T(4,128)S(1)} collective-permute-done((f32[3,192]{1,0:T(4,128)S(1)}, f32[3,192]{1,0:T(4,128)S(1)}, u32[]{:S(2)}, u32[]{:S(2)}) %collective-permute-start.3) | collective-permute-done | bytes 2336 | tf_op jit(solution)/shard_map/ppermute | solution.py:47
  120.7 4.3 %collective-permute-start.4 = (f32[3,192]{1,0:T(4,128)S(1)}, f32[3,192]{1,0:T(4,128)S(1)}, u32[]{:S(2)}, u32[]{:S(2)}) collective-permute-start(f32[3,192]{1,0:T(4,128)S(1)} %pad_maximum_fusion.4), channel_id=1, source_target_pairs={{0,32},{8,40},{16,48},{24,56},{32,0},{40,8},{48,16},{56,24},{64,96... | collective-permute-start | bytes 6920 | tf_op jit(solution)/shard_map/ppermute | solution.py:47
  125.1 1.6 collective-permute-done.4
  126.7 1.7 collective-permute-start.5
  128.4 2.0 collective-permute-done.5
  130.5 3.2 %collective-permute-start.6 = (f32[3,192]{1,0:T(4,128)S(1)}, f32[3,192]{1,0:T(4,128)S(1)}, u32[]{:S(2)}, u32[]{:S(2)}) collective-permute-start(f32[3,192]{1,0:T(4,128)S(1)} %pad_maximum_fusion.6), channel_id=1, source_target_pairs={{0,128},{8,136},{16,144},{24,152},{32,160},{40,168},{48,176},{56,1... | collective-permute-start | bytes 6920 | tf_op jit(solution)/shard_map/ppermute | solution.py:47
  133.7 2.2 collective-permute-done.6
  136.0 2.9 fusion.18
  138.8 0.0 reduce-scatter.3.cloned.1.call-update
  138.8 0.0 all-gather.8.cloned.1.call-start
  138.9 44.0 %reduce-scatter.3.cloned.1.call-done = bf16[128,1536]{1,0:T(8,128)(2,1)} async-done(((bf16[1024,1536]{1,0:T(8,128)(2,1)}), bf16[128,1536]{1,0:T(8,128)(2,1)}) %reduce-scatter.3.cloned.1.call-update) | async-done | bytes 393232 | tf_op jit(solution)/shard_map/reduce_scatter | solution.py:104
  182.9 1.2 convert_reduce_fusion
  184.1 0.3 fusion.10
  184.4 1.0 fusion.12
  185.4 0.0 all-gather.8.cloned.1.call-update
  185.4 0.0 reduce-scatter.5.cloned.1.call-start
  185.5 44.6 %all-gather.8.cloned.1.call-done = bf16[1024,1536]{1,0:T(8,128)(2,1)} async-done(((bf16[128,1536]{1,0:T(8,128)(2,1)}), bf16[1024,1536]{1,0:T(8,128)(2,1)}) %all-gather.8.cloned.1.call-update) | async-done | bytes 3145744 | tf_op jit(solution)/shard_map/all_gather | solution.py:109
  230.0 11.0 %convolution_convert_fusion = bf16[1024,1536]{1,0:T(8,128)(2,1)} fusion(bf16[768,1536]{0,1:T(8,128)(2,1)} %all-gather.6.cloned.1.call-done, bf16[1024,1536]{1,0:T(8,128)(2,1)} %all-gather.8.cloned.1.call-done, bf16[1536,768]{1,0:T(8,128)(2,1)} %all-gather.4.cloned.1.call-done), kind=kOutput, calls=%fused_computation | convolution fusion | flops 4837343232 | bytes 11010048 | tf_op jit(solution)/shard_map/dot_general | solution.py:112
  241.1 0.0 reduce-scatter.5.cloned.1.call-update
  241.1 45.6 %reduce-scatter.5.cloned.1.call-done = bf16[128,1536]{1,0:T(8,128)(2,1)} async-done(((bf16[1024,1536]{1,0:T(8,128)(2,1)}), bf16[128,1536]{1,0:T(8,128)(2,1)}) %reduce-scatter.5.cloned.1.call-update) | async-done | bytes 393232 | tf_op jit(solution)/shard_map/reduce_scatter | solution.py:113
  286.7 1.9 fusion.17
  (45 shorter events, 0.3 us)
Async XLA Ops:
  6.5 129.4 %copy-start = (bf16[192,1536]{1,0:T(8,128)(2,1)S(1)}, bf16[192,1536]{1,0:T(8,128)(2,1)}, u32[]{:S(2)}) copy-start(bf16[192,1536]{1,0:T(8,128)(2,1)} %param.22) | copy-start | bytes 1769476
  12.2 10.8 %copy-start.4 = (s32[1024]{0:T(1024)S(1)}, s32[1024]{0:T(1024)}, u32[]{:S(2)}) copy-start(s32[1024]{0:T(1024)} %param.14) | copy-start | bytes 12292
  12.2 11.5 %copy-start.2 = (f32[31,192]{1,0:T(8,128)S(1)}, f32[31,192]{1,0:T(8,128)}, u32[]{:S(2)}) copy-start(f32[31,192]{1,0:T(8,128)} %param.19) | copy-start | bytes 71428
  12.2 82.5 %copy-start.5 = (bf16[1536,192]{0,1:T(8,128)(2,1)S(1)}, bf16[1536,192]{0,1:T(8,128)(2,1)}, u32[]{:S(2)}) copy-start(bf16[1536,192]{0,1:T(8,128)(2,1)} %param.18) | copy-start | bytes 1769476
  12.2 82.5 %all-to-all-start = ((bf16[8,128,1536]{2,1,0:T(8,128)(2,1)}), bf16[8,128,1536]{2,1,0:T(8,128)(2,1)}, u32[]{:S(2)}, u32[]{:S(2)}) async-start(bf16[8,128,1536]{2,1,0:T(8,128)(2,1)} %tile.2), calls=%async_computation | async-start | bytes 6291456 | tf_op jit(solution)/shard_map/all_to_all | solution.py:81
  20.8 118.0 %all-gather.4.cloned.1.call-start = ((), (), s32[]{:S(2)}) async-start(), calls=%async_computation.3 | async-start | bytes 2433024 | tf_op jit(solution)/shard_map/all_gather | solution.py:82
  21.6 117.3 %all-gather.6.cloned.1.call-start = ((), (), s32[]{:S(2)}) async-start(), calls=%async_computation.4 | async-start | bytes 2433024 | tf_op jit(solution)/shard_map/all_gather | solution.py:83
  22.3 160.6 %reduce-scatter.3.cloned.1.call-start = ((), (), s32[]{:S(2)}) async-start(), calls=%async_computation.5 | async-start | bytes 3538944 | tf_op jit(solution)/shard_map/reduce_scatter | solution.py:104
  94.7 3.2 %copy-start.6 = (bf16[1536,192]{0,1:T(8,128)(2,1)S(1)}, bf16[1536,192]{0,1:T(8,128)(2,1)}, u32[]{:S(2)}) copy-start(bf16[1536,192]{0,1:T(8,128)(2,1)} %param.17) | copy-start | bytes 1769476
  97.9 38.0 %copy-start.7 = (f32[192]{0:T(256)S(1)}, f32[192]{0:T(256)}, u32[]{:S(2)}) copy-start(f32[192]{0:T(256)} %param.21) | copy-start | bytes 2308
  97.9 38.0 %copy-start.8 = (f32[192]{0:T(256)S(1)}, f32[192]{0:T(256)}, u32[]{:S(2)}) copy-start(f32[192]{0:T(256)} %param.20) | copy-start | bytes 2308
  101.1 7.6 %collective-permute-start = (bf16[15,192]{0,1:T(8,128)(2,1)S(1)}, bf16[15,192]{0,1:T(8,128)(2,1)S(1)}, u32[]{:S(2)}, u32[]{:S(2)}) collective-permute-start(bf16[15,192]{0,1:T(8,128)(2,1)S(1)} %get-tuple-element.31), channel_id=1, source_target_pairs={{0,8},{8,16},{16,24},{24,32},{32,40},{40,48},{48,56},{56,64},{64,7... | collective-permute-start | bytes 17288 | tf_op jit(solution)/shard_map/ppermute | solution.py:17
  103.1 5.7 %collective-permute-start.1 = (bf16[15,192]{0,1:T(8,128)(2,1)S(1)}, bf16[15,192]{0,1:T(8,128)(2,1)S(1)}, u32[]{:S(2)}, u32[]{:S(2)}) collective-permute-start(bf16[15,192]{0,1:T(8,128)(2,1)S(1)} %get-tuple-element.32), channel_id=1, source_target_pairs={{8,0},{16,8},{24,16},{32,24},{40,32},{48,40},{56,48},{64,56},{72,6... | collective-permute-start | bytes 17288 | tf_op jit(solution)/shard_map/ppermute | solution.py:18
  114.7 2.1 collective-permute-start.2
  117.0 3.7 %collective-permute-start.3 = (f32[3,192]{1,0:T(4,128)S(1)}, f32[3,192]{1,0:T(4,128)S(1)}, u32[]{:S(2)}, u32[]{:S(2)}) collective-permute-start(f32[3,192]{1,0:T(4,128)S(1)} %pad_maximum_fusion.3), channel_id=1, source_target_pairs={{0,16},{8,24},{16,0},{24,8},{32,48},{40,56},{48,32},{56,40},{64,80... | collective-permute-start | bytes 6920 | tf_op jit(solution)/shard_map/ppermute | solution.py:47
  120.7 5.9 %collective-permute-start.4 = (f32[3,192]{1,0:T(4,128)S(1)}, f32[3,192]{1,0:T(4,128)S(1)}, u32[]{:S(2)}, u32[]{:S(2)}) collective-permute-start(f32[3,192]{1,0:T(4,128)S(1)} %pad_maximum_fusion.4), channel_id=1, source_target_pairs={{0,32},{8,40},{16,48},{24,56},{32,0},{40,8},{48,16},{56,24},{64,96... | collective-permute-start | bytes 6920 | tf_op jit(solution)/shard_map/ppermute | solution.py:47
  126.7 3.7 %collective-permute-start.5 = (f32[3,192]{1,0:T(4,128)S(1)}, f32[3,192]{1,0:T(4,128)S(1)}, u32[]{:S(2)}, u32[]{:S(2)}) collective-permute-start(f32[3,192]{1,0:T(4,128)S(1)} %pad_maximum_fusion.5), channel_id=1, source_target_pairs={{0,64},{8,72},{16,80},{24,88},{32,96},{40,104},{48,112},{56,120},{... | collective-permute-start | bytes 6920 | tf_op jit(solution)/shard_map/ppermute | solution.py:47
  130.5 5.4 %collective-permute-start.6 = (f32[3,192]{1,0:T(4,128)S(1)}, f32[3,192]{1,0:T(4,128)S(1)}, u32[]{:S(2)}, u32[]{:S(2)}) collective-permute-start(f32[3,192]{1,0:T(4,128)S(1)} %pad_maximum_fusion.6), channel_id=1, source_target_pairs={{0,128},{8,136},{16,144},{24,152},{32,160},{40,168},{48,176},{56,1... | collective-permute-start | bytes 6920 | tf_op jit(solution)/shard_map/ppermute | solution.py:47
  138.8 44.1 %copy-start.1 = (bf16[128,1536]{1,0:T(8,128)(2,1)S(1)}, bf16[128,1536]{1,0:T(8,128)(2,1)}, u32[]{:S(2)}) copy-start(bf16[128,1536]{1,0:T(8,128)(2,1)} %param.13) | copy-start | bytes 1179652
  138.8 45.5 %copy-start.3 = (f32[1536]{0:T(1024)S(1)}, f32[1536]{0:T(1024)}, u32[]{:S(2)}) copy-start(f32[1536]{0:T(1024)} %param.23) | copy-start | bytes 18436
  138.8 91.2 %all-gather.8.cloned.1.call-start = ((), (), s32[]{:S(2)}) async-start(), calls=%async_computation.6 | async-start | bytes 3538944 | tf_op jit(solution)/shard_map/all_gather | solution.py:109
  185.4 101.3 %reduce-scatter.5.cloned.1.call-start = ((), (), s32[]{:S(2)}) async-start(), calls=%async_computation.7 | async-start | bytes 3538944 | tf_op jit(solution)/shard_map/reduce_scatter | solution.py:113
Sparse Core Ops, SparseCore 0:
  24.2 50.4 all-gather.3
  77.2 48.6 all-gather.5
  139.0 43.8 reduce-scatter.2
  185.5 44.4 all-gather.7
  241.2 45.4 reduce-scatter.4
